TPU v7x, 256 devices: a whole 4x4x8 slice. The times are simulated.
256 devices in a mesh: dp: 4 (over x), ctx: 16 (over z, y_hi), tp: 4 (over y_lo, core).
Axes of the slice: x: 4, y: 4 (y_hi: 2, y_lo: 2; y = y_hi * 2 + y_lo), z: 8, core: 2. Of those that a mesh axis runs over, the one named last changes fastest.
Arguments:
- query_rows: bfloat16 [16384, 4096], P(('dp', 'ctx'), 'tp'), parts along dimension 0, may hold values from -6 to 6
- key_matrix: bfloat16 [16384, 512], P(('dp', 'ctx'), 'tp'), parts along dimension 0, may hold values from -6 to 6
- value_matrix: bfloat16 [16384, 512], P(('dp', 'ctx'), 'tp'), parts along dimension 0, may hold values from -6 to 6
- attn_out: bfloat16 [16384, 4096], P(('dp', 'ctx'), 'tp'), parts along dimension 0, may hold values from -6 to 6
- out_grad: bfloat16 [16384, 4096], P(('dp', 'ctx', 'tp')), parts along dimension 0, may hold values from -0.5 to 0.5
- log_sums: float32 [32, 16384], P('tp', ('dp', 'ctx')), parts along dimension 1, may hold values from 3 to 5
- block_mask: int32 [128, 32], P('dp'), parts along dimension 0, may hold values 0 or 1
Outputs:
- query_grad: bfloat16 [16384, 4096], P(('dp', 'ctx'), 'tp'), parts along dimension 0
- key_gradient: bfloat16 [16384, 512], P(('dp', 'ctx'), 'tp'), parts along dimension 0
- value_gradient: bfloat16 [16384, 512], P(('dp', 'ctx'), 'tp'), parts along dimension 0
There are 4 independent parts, one for each index of `dp`. A program takes and returns all parts, laid end to end along the dimension named above; each array names one. Nothing has to cross between parts.
Inputs may be any that keep to these rules, and one draw needn't show every extreme that they name: `block_mask`: entry [a, b] with b < a lets query block a see key block b; entries on and above the diagonal are never read.
All inputs are finite; a program needn't handle non-finite values.
Results may differ from a plain program's by a relative error of at most 0.0049.
Values may be sent and summed in bfloat16 or wider, within the bound.
No kernel may reach another device: no remote copies, remote signals or barrier semaphores. Data moves between devices by JAX's collectives and lax.ppermute only.
A program may use at most 64 MiB of HBM per device.

v0:
```python
import math
import jax
import jax.numpy as jnp
from jax import lax
from jax.sharding import PartitionSpec as P

BLK = 128
HEAD_SIZE = 128


def live_region(block_mask, query_start, tok_rows, key_start, key_count):
    block_table = lax.dynamic_slice(
        block_mask, (query_start // BLK, key_start // BLK), (tok_rows // BLK, key_count // BLK)
    )
    block_table = jnp.repeat(jnp.repeat(block_table, BLK, axis=0), BLK, axis=1)
    query_pos = query_start + jnp.arange(tok_rows, dtype=jnp.int32)
    key_pos = key_start + jnp.arange(key_count, dtype=jnp.int32)
    query_block = (query_pos // BLK)[:, None]
    key_block = (key_pos // BLK)[None, :]
    earlier = (key_block < query_block) & (block_table == 1)
    diagonal = (key_block == query_block) & (key_pos[None, :] <= query_pos[:, None])
    return earlier | diagonal


def contract(queries, out_grads, row_delta, log_sums, keys_part, values_part, live_mask):
    logit_scale = 1.0 / math.sqrt(HEAD_SIZE)
    scores = (
        jnp.einsum("igd,jd->gij", queries, keys_part, preferred_element_type=jnp.float32)
        * logit_scale
    )
    probabilities = jnp.where(live_mask[None], jnp.exp(scores - log_sums[:, :, None]), 0.0)
    prob_grad = jnp.einsum(
        "igd,jd->gij", out_grads, values_part, preferred_element_type=jnp.float32
    )
    dscore = (probabilities * (prob_grad - row_delta[:, :, None])).astype(jnp.bfloat16)
    query_term = jnp.einsum("gij,jd->igd", dscore, keys_part, preferred_element_type=jnp.float32)
    key_term = jnp.einsum("gij,igd->jd", dscore, queries, preferred_element_type=jnp.float32)
    value_term = jnp.einsum(
        "gij,igd->jd",
        probabilities.astype(jnp.bfloat16),
        out_grads,
        preferred_element_type=jnp.float32,
    )
    return (query_term, key_term, value_term)


def local(query_rows, key_matrix, value_matrix, attn_out, out_grad, log_sums, block_mask):
    tok_rows = query_rows.shape[0]
    col_width = query_rows.shape[1]
    heads_local = col_width // HEAD_SIZE
    ctx_pos = lax.axis_index("ctx")
    ctx_count = lax.axis_size("ctx")
    tp_count = lax.axis_size("tp")
    grad_rows = out_grad.shape[0]
    pieces = out_grad.reshape(grad_rows, tp_count, col_width)
    own_grad = lax.all_to_all(pieces, "tp", split_axis=1, concat_axis=0, tiled=True)
    own_grad = own_grad.reshape(tok_rows, col_width)
    queries = query_rows.reshape(tok_rows, heads_local, HEAD_SIZE)
    out_grads = own_grad.reshape(tok_rows, heads_local, HEAD_SIZE)
    outputs = attn_out.reshape(tok_rows, heads_local, HEAD_SIZE)
    row_delta = jnp.sum(out_grads.astype(jnp.float32) * outputs.astype(jnp.float32), axis=2).T
    query_start = ctx_pos * tok_rows
    key_values = jnp.concatenate([key_matrix, value_matrix], axis=1)
    all_key_values = lax.all_gather(key_values, "ctx", axis=0, tiled=True)
    zero_query = jnp.zeros((tok_rows, heads_local, HEAD_SIZE), jnp.float32)
    zero_partial = jnp.zeros((ctx_count * tok_rows, 2 * HEAD_SIZE), jnp.float32)

    def visit_span(span, carried):
        query_acc, partial = carried
        key_start = span * tok_rows
        span_kv = lax.dynamic_slice_in_dim(all_key_values, key_start, tok_rows, 0)
        keys_part = span_kv[:, :HEAD_SIZE]
        values_part = span_kv[:, HEAD_SIZE:]
        live_mask = live_region(block_mask, query_start, tok_rows, key_start, tok_rows)
        query_term, key_term, value_term = contract(
            queries, out_grads, row_delta, log_sums, keys_part, values_part, live_mask
        )
        span_partial = jnp.concatenate([key_term, value_term], axis=1)
        partial = lax.dynamic_update_slice_in_dim(partial, span_partial, key_start, 0)
        return (query_acc + query_term, partial)

    query_acc, partial = lax.fori_loop(0, ctx_pos + 1, visit_span, (zero_query, zero_partial))
    summed = lax.psum_scatter(partial, "ctx", scatter_dimension=0, tiled=True)
    logit_scale = 1.0 / math.sqrt(HEAD_SIZE)
    query_grad = (query_acc * logit_scale).reshape(tok_rows, col_width).astype(jnp.bfloat16)
    key_gradient = (summed[:, :HEAD_SIZE] * logit_scale).astype(jnp.bfloat16)
    value_gradient = summed[:, HEAD_SIZE:].astype(jnp.bfloat16)
    return (query_grad, key_gradient, value_gradient)


def solution(mesh):
    placed = (
        P(("dp", "ctx"), "tp"),
        P(("dp", "ctx"), "tp"),
        P(("dp", "ctx"), "tp"),
        P(("dp", "ctx"), "tp"),
        P(("dp", "ctx", "tp"), None),
        P("tp", ("dp", "ctx")),
        P("dp", None),
    )
    return jax.shard_map(
        local,
        mesh=mesh,
        in_specs=placed,
        out_specs=(P(("dp", "ctx"), "tp"), P(("dp", "ctx"), "tp"), P(("dp", "ctx"), "tp")),
        check_vma=False,
    )
```

profile of v0, /device:TPU:4, one launch (start us, length us, event | category | flops | bytes accessed | tf_op | source)
XLA Modules:
  0.0 429.3 jit_solution(2428679739724852573)
XLA Ops:
  7.2 0.0 copy-start.1
  7.2 0.0 copy-start
  7.2 0.0 all-gather.2.cloned.1.call-start
  7.2 1.6 pad_maximum_fusion.1
  8.8 0.0 all-gather.2.cloned.1.call-update
  8.9 1.9 copy.66
  10.7 3.5 all-to-all-start
  14.2 0.0 reduce-scatter.2.cloned.1.call-start
  14.3 0.0 copy-done.1
  14.3 0.2 copy.40
  14.5 0.0 copy-done
  14.5 0.1 convert_bitcast_fusion
  14.6 0.2 copy.62
  14.8 8.2 %all-to-all-done = bf16[64,4,1024]{2,0,1:T(8,128)(2,1)S(1)} async-done(((bf16[64,4,1024]{2,0,1:T(8,128)(2,1)}), bf16[64,4,1024]{2,0,1:T(8,128)(2,1)S(1)}, u32[]{:S(2)}, u32[]{:S(2)}) %all-to-all-start) | async-done | bytes 524320 | tf_op jit(solution)/shard_map/all_to_all | solution.py:56
  23.0 0.1 copy.61
  23.1 0.3 copy.43
  23.5 0.3 multiply_reduce_fusion
  23.8 0.1 copy.44
  23.9 75.2 %all-gather.2.cloned.1.call-done = bf16[4096,256]{1,0:T(8,128)(2,1)} async-done(((bf16[256,256]{1,0:T(8,128)(2,1)}), bf16[4096,256]{1,0:T(8,128)(2,1)}) %all-gather.2.cloned.1.call-update) | async-done | bytes 2097168 | tf_op jit(solution)/shard_map/all_gather | solution.py:64
  99.1 0.1 broadcast_in_dim.48
  99.2 0.0 copy-start.2
  99.2 2.2 broadcast_in_dim.49.clone
  101.4 0.0 copy-done.2
  101.4 6.9 %while.15 = (s32[]{:T(128)}, f32[256,8,128]{0,2,1:T(8,128)S(1)}, f32[4096,256]{1,0:T(8,128)}, s32[]{:T(128)}, bf16[4096,256]{1,0:T(8,128)(2,1)}, /*index=5*/s32[...) while((s32[]{:T(128)}, f32[256,8,128]{0,2,1:T(8,128)S(1)}, ...), condition=%wide.region_2.3_spmd, body=%wide.region_1.2_spmd.sunk | while | flops 675487744 | bytes 15821342 | solution.py:82
  101.4 0.8 dynamic_slice.15
  102.2 0.1 copy.70
  102.3 0.1 broadcast_bitcast_fusion.2
  102.4 0.2 fusion.34
  102.6 1.4 fusion.35
  104.0 0.5 convolution_bitcast_fusion.5
  104.5 1.3 fusion.36
  105.7 0.5 convolution_bitcast_fusion.6
  106.2 1.2 fusion.37
  107.5 0.1 copy.72
  107.6 0.7 constant_dynamic-update-slice_fusion.2
  108.3 0.0 reduce-scatter.2.cloned.1.call-update
  108.3 0.1 multiply_convert_fusion
  108.4 1.0 copy.54
  109.4 309.9 %reduce-scatter.2.cloned.1.call-done = f32[256,256]{1,0:T(8,128)} async-done(((f32[4096,256]{1,0:T(8,128)}), f32[256,256]{1,0:T(8,128)}) %reduce-scatter.2.cloned.1.call-update) | async-done | bytes 262160 | tf_op jit(solution)/shard_map/reduce_scatter | solution.py:83
  419.3 1.5 slice.29
  420.9 1.5 fusion.9
  (5 shorter events, 0.1 us)
Async XLA Ops:
  7.2 7.1 %copy-start.1 = (bf16[256,1024]{1,0:T(8,128)(2,1)S(1)}, bf16[256,1024]{1,0:T(8,128)(2,1)}, u32[]{:S(2)}) copy-start(bf16[256,1024]{1,0:T(8,128)(2,1)} %param.9) | copy-start | bytes 1572868
  7.2 7.3 %copy-start = (bf16[256,1024]{1,0:T(8,128)(2,1)S(1)}, bf16[256,1024]{1,0:T(8,128)(2,1)}, u32[]{:S(2)}) copy-start(bf16[256,1024]{1,0:T(8,128)(2,1)} %param.12) | copy-start | bytes 1572868
  7.2 91.9 %all-gather.2.cloned.1.call-start = ((), (), s32[]{:S(2)}) async-start(), calls=%async_computation.2 | async-start | bytes 2228224 | tf_op jit(solution)/shard_map/all_gather | solution.py:64
  10.7 12.3 %all-to-all-start = ((bf16[64,4,1024]{2,0,1:T(8,128)(2,1)}), bf16[64,4,1024]{2,0,1:T(8,128)(2,1)S(1)}, u32[]{:S(2)}, u32[]{:S(2)}) async-start(bf16[64,4,1024]{2,0,1:T(8,128)(2,1)} %bitcast.62), calls=%async_computation | async-start | bytes 1048576 | tf_op jit(solution)/shard_map/all_to_all | solution.py:56
  14.2 405.1 %reduce-scatter.2.cloned.1.call-start = ((), (), s32[]{:S(2)}) async-start(), calls=%async_computation.3 | async-start | bytes 4456448 | tf_op jit(solution)/shard_map/reduce_scatter | solution.py:83
  99.2 2.2 copy-start.2
Sparse Core Ops, SparseCore 0:
  10.6 88.4 all-gather.1
  108.5 310.8 reduce-scatter.1
where the time goes:
time: 432 us; the launch traced here: 429 us
  waiting for transfers between devices  393 us (91%)
  between operations  14.2 us (3%)
  local copies, waits for them, and re-layouts  9.4 us (2%)
  matrix products  4.83 us (1%)
    reduce_scatter x1, waiting for transfers between devices, local(): summed = lax.psum_scatter(partial, 'ctx', scatter_dimension=0, tiled=True)  310 us
    all_gather x1, waiting for transfers between devices, local(): all_key_values = lax.all_gather(key_values, 'ctx', axis=0, tiled=True)  75.2 us
  transfers between devices with their start and end apart: 3, of which 3 were waited for; matrix products, arithmetic and copies ran while one was open for 1% of the time, Pallas kernels for 0%

commit v1 on v0

--- a/solution.py
+++ b/solution.py
@@ -61,7 +61,9 @@
     row_delta = jnp.sum(out_grads.astype(jnp.float32) * outputs.astype(jnp.float32), axis=2).T
     query_start = ctx_pos * tok_rows
     key_values = jnp.concatenate([key_matrix, value_matrix], axis=1)
-    all_key_values = lax.all_gather(key_values, "ctx", axis=0, tiled=True)
+    all_key_values = jnp.concatenate(
+        lax.all_to_all(jnp.stack([key_values] * lax.axis_size("ctx")), "ctx", 0, 0), axis=0
+    )
     zero_query = jnp.zeros((tok_rows, heads_local, HEAD_SIZE), jnp.float32)
     zero_partial = jnp.zeros((ctx_count * tok_rows, 2 * HEAD_SIZE), jnp.float32)
 

time: 432 us -> 417 us (0.965)
  waiting for transfers between devices: 393 us -> 367 us
  starting transfers between devices: 3.55 us -> 14.9 us
    all_gather x1 -> x0, waiting for transfers between devices: 75.2 us -> none  [local(): all_key_values = lax.all_gather(key_values, 'ctx', axis=0, tiled=True)]
    all_to_all x0 -> x1, waiting for transfers between devices: none -> 50.4 us  [local(): lax.all_to_all(jnp.stack([key_values] * lax.axis_size('ctx')), 'ctx', 0, 0)]
    all_to_all x0 -> x1, starting transfers between devices: none -> 11.4 us  [local(): lax.all_to_all(jnp.stack([key_values] * lax.axis_size('ctx')), 'ctx', 0, 0)]
where the time goes in v1:
time: 417 us; the launch traced here: 414 us
  waiting for transfers between devices  367 us (88%)
  starting transfers between devices  14.9 us (4%)
  between operations  14.2 us (3%)
  local copies, waits for them, and re-layouts  11 us (3%)
  matrix products  4.83 us (1%)
    reduce_scatter x1, waiting for transfers between devices, local(): summed = lax.psum_scatter(partial, 'ctx', scatter_dimension=0, tiled=True)  308 us
    all_to_all x1, waiting for transfers between devices, local(): lax.all_to_all(jnp.stack([key_values] * lax.axis_size('ctx')), 'ctx', 0, 0)  50.4 us
    all_to_all x1, starting transfers between devices, local(): lax.all_to_all(jnp.stack([key_values] * lax.axis_size('ctx')), 'ctx', 0, 0)  11.4 us
    all_to_all x1, waiting for transfers between devices, local(): lax.all_to_all(pieces, 'tp', split_axis=1, concat_axis=0, tiled=True)  8.77 us
  transfers between devices with their start and end apart: 3, of which 3 were waited for; matrix products, arithmetic and copies ran while one was open for 1% of the time, Pallas kernels for 0%

profile of v1, /device:TPU:4, one launch (start us, length us, event | category | flops | bytes accessed | tf_op | source)
XLA Modules:
  0.0 414.2 jit_solution(5802424766093783550)
XLA Ops:
  7.2 0.0 copy-start.2
  7.2 0.0 copy-start.3
  7.2 1.9 copy.66
  9.1 3.5 all-to-all-start.1
  12.6 0.0 copy-done.2
  12.6 0.0 copy-done.3
  12.6 8.8 %all-to-all-done.1 = bf16[64,4,1024]{2,0,1:T(8,128)(2,1)S(1)} async-done(((bf16[64,4,1024]{2,0,1:T(8,128)(2,1)}), bf16[64,4,1024]{2,0,1:T(8,128)(2,1)S(1)}, u32[]{:S(2)}, u32[]{:S(2)}) %all-to-all-start.1) | async-done | bytes 524320 | tf_op jit(solution)/shard_map/all_to_all | solution.py:56
  21.4 1.5 stack.2
  22.9 0.0 copy-start.1
  22.9 0.0 copy-start
  22.9 11.4 %all-to-all-start = ((bf16[16,256,256]{2,1,0:T(8,128)(2,1)}), bf16[16,256,256]{2,1,0:T(8,128)(2,1)}, u32[]{:S(2)}, u32[]{:S(2)}) async-start(bf16[16,256,256]{2,1,0:T(8,128)(2,1)} %stack.2), calls=%async_computation | async-start | bytes 4194304 | tf_op jit(solution)/shard_map/all_to_all | solution.py:65
  34.3 0.0 reduce-scatter.2.cloned.1.call-start
  34.4 0.0 copy-done.1
  34.4 0.2 copy.40
  34.6 0.0 copy-done
  34.6 0.1 convert_bitcast_fusion
  34.7 0.2 copy.62
  34.9 0.1 copy.61
  35.0 0.3 copy.43
  35.4 0.3 multiply_reduce_fusion
  35.7 0.1 copy.44
  35.8 50.4 %all-to-all-done = bf16[16,256,256]{2,1,0:T(8,128)(2,1)} async-done(((bf16[16,256,256]{2,1,0:T(8,128)(2,1)}), bf16[16,256,256]{2,1,0:T(8,128)(2,1)}, u32[]{:S(2)}, u32[]{:S(2)}) %all-to-all-start) | async-done | bytes 2097184 | tf_op jit(solution)/shard_map/all_to_all | solution.py:65
  86.2 0.1 broadcast_in_dim.48
  86.2 0.0 copy-start.4
  86.3 2.2 broadcast_in_dim.49.clone
  88.5 0.0 copy-done.4
  88.5 6.9 %while.15 = (s32[]{:T(128)}, f32[256,8,128]{0,2,1:T(8,128)S(1)}, f32[4096,256]{1,0:T(8,128)}, s32[]{:T(128)}, bf16[4096,256]{1,0:T(8,128)(2,1)}, /*index=5*/s32[...) while((s32[]{:T(128)}, f32[256,8,128]{0,2,1:T(8,128)S(1)}, ...), condition=%wide.region_2.3_spmd, body=%wide.region_1.2_spmd.sunk | while | flops 675487744 | bytes 15821342 | solution.py:84
  88.5 0.8 dynamic_slice.15
  89.3 0.1 copy.70
  89.4 0.1 broadcast_bitcast_fusion.2
  89.5 0.2 fusion.34
  89.6 1.4 fusion.35
  91.1 0.5 convolution_bitcast_fusion.5
  91.5 1.3 fusion.36
  92.8 0.5 convolution_bitcast_fusion.6
  93.3 1.2 fusion.37
  94.5 0.1 copy.72
  94.7 0.7 constant_dynamic-update-slice_fusion.2
  95.4 0.0 reduce-scatter.2.cloned.1.call-update
  95.4 0.1 multiply_convert_fusion
  95.5 1.0 copy.54
  96.5 307.7 %reduce-scatter.2.cloned.1.call-done = f32[256,256]{1,0:T(8,128)} async-done(((f32[4096,256]{1,0:T(8,128)}), f32[256,256]{1,0:T(8,128)}) %reduce-scatter.2.cloned.1.call-update) | async-done | bytes 262160 | tf_op jit(solution)/shard_map/reduce_scatter | solution.py:85
  404.2 1.5 slice.29
  405.8 1.5 fusion.9
  (6 shorter events, 0.1 us)
Async XLA Ops:
  7.2 5.4 %copy-start.2 = (bf16[256,128]{1,0:T(8,128)(2,1)S(1)}, bf16[256,128]{1,0:T(8,128)(2,1)}, u32[]{:S(2)}) copy-start(bf16[256,128]{1,0:T(8,128)(2,1)} %param.11) | copy-start | bytes 196612
  7.2 5.4 %copy-start.3 = (bf16[256,128]{1,0:T(8,128)(2,1)S(1)}, bf16[256,128]{1,0:T(8,128)(2,1)}, u32[]{:S(2)}) copy-start(bf16[256,128]{1,0:T(8,128)(2,1)} %param.10) | copy-start | bytes 196612
  9.1 12.3 %all-to-all-start.1 = ((bf16[64,4,1024]{2,0,1:T(8,128)(2,1)}), bf16[64,4,1024]{2,0,1:T(8,128)(2,1)S(1)}, u32[]{:S(2)}, u32[]{:S(2)}) async-start(bf16[64,4,1024]{2,0,1:T(8,128)(2,1)} %bitcast.63), calls=%async_computation.1 | async-start | bytes 1048576 | tf_op jit(solution)/shard_map/all_to_all | solution.py:56
  22.9 11.5 %copy-start.1 = (bf16[256,1024]{1,0:T(8,128)(2,1)S(1)}, bf16[256,1024]{1,0:T(8,128)(2,1)}, u32[]{:S(2)}) copy-start(bf16[256,1024]{1,0:T(8,128)(2,1)} %param.9) | copy-start | bytes 1572868
  22.9 11.7 %copy-start = (bf16[256,1024]{1,0:T(8,128)(2,1)S(1)}, bf16[256,1024]{1,0:T(8,128)(2,1)}, u32[]{:S(2)}) copy-start(bf16[256,1024]{1,0:T(8,128)(2,1)} %param.12) | copy-start | bytes 1572868
  22.9 63.2 %all-to-all-start = ((bf16[16,256,256]{2,1,0:T(8,128)(2,1)}), bf16[16,256,256]{2,1,0:T(8,128)(2,1)}, u32[]{:S(2)}, u32[]{:S(2)}) async-start(bf16[16,256,256]{2,1,0:T(8,128)(2,1)} %stack.2), calls=%async_computation | async-start | bytes 4194304 | tf_op jit(solution)/shard_map/all_to_all | solution.py:65
  34.3 369.9 %reduce-scatter.2.cloned.1.call-start = ((), (), s32[]{:S(2)}) async-start(), calls=%async_computation.3 | async-start | bytes 4456448 | tf_op jit(solution)/shard_map/reduce_scatter | solution.py:85
  86.2 2.2 copy-start.4
Sparse Core Ops, SparseCore 0:
  95.5 308.6 reduce-scatter.1
